TPU v7x, 32 devices: a whole 2x2x4 slice. The times are simulated.
32 devices in a mesh: blk: 16 (over z, y, x), band: 2 (over core).
Axes of the slice: x: 2, y: 2, z: 4, core: 2. Of those that a mesh axis runs over, the one named last changes fastest.
Arguments:
- traces: bfloat16 [1024, 2, 8192], P('blk', None, 'band'), may hold values from -80 to 80
- sources: bfloat16 [32, 2, 8192], P('blk', None, 'band'), may hold values from -80 to 80
- owner: int32 [1024, 1], P('blk'), may hold values from 0 to 15; in each aligned block of 64 rows (0 to 63, 64 to 127, ...) at most 8 rows name the same one
Outputs:
- gathers: float32 [32, 4, 128, 256], P('blk', None, 'band')
Inputs may be any that keep to these rules, and one draw needn't show every extreme that they name: Among the 64 stations of one device's rows, at most 8 name the same owner block, and some owner block is named by exactly 8 of them in every draw.
All inputs are finite; a program needn't handle non-finite values.
Results may differ from a plain program's by a relative error of at most 0.017.
Values may be sent and summed in bfloat16 or wider, within the bound.
No kernel may reach another device: no remote copies, remote signals or barrier semaphores. Data moves between devices by JAX's collectives and lax.ppermute only.
A program may use at most 128 MiB of HBM per device.

v0:
```python
import math
import jax
import jax.numpy as jnp
from jax import lax
from jax.sharding import PartitionSpec as P

BINS = 8192
LAGS = 2048
DEC = 8
PERIOD = BINS // DEC
EPS = 1e-06


def per_device(traces, sources, owner):
    blocks = lax.axis_size("blk")
    station_count = traces.shape[0]
    source_count = sources.shape[0]
    group_bins = traces.shape[2]
    folds = group_bins // PERIOD
    capacity = max(2, 2 * station_count // blocks)
    lags_out = LAGS // DEC
    offsets = blocks // 4
    all_sources = lax.all_gather(sources, "blk", axis=0, tiled=True)
    trace_float = traces.astype(jnp.float32)
    all_source_float = all_sources.astype(jnp.float32)
    trace_power, source_power = lax.psum(
        (
            jnp.sum(trace_float * trace_float, axis=(1, 2)),
            jnp.sum(all_source_float * all_source_float, axis=(1, 2)),
        ),
        "band",
    )
    white_traces = (
        (trace_float * lax.rsqrt(trace_power / (2 * BINS) + EPS)[:, None, None])
        .astype(jnp.bfloat16)
        .reshape(station_count, 2 * group_bins)
    )
    white_sources = (
        (all_source_float * lax.rsqrt(source_power / (2 * BINS) + EPS)[:, None, None])
        .astype(jnp.bfloat16)
        .astype(jnp.float32)
        .reshape(blocks, source_count, 2, folds, PERIOD)
    )
    owners = owner[:, 0]
    owner_hits = (owners[:, None] == jnp.arange(blocks, dtype=jnp.int32)[None, :]).astype(jnp.int32)
    earlier = jnp.cumsum(owner_hits, axis=0) - owner_hits
    arrival = jnp.sum(owner_hits * earlier, axis=1)
    slot_index = owners * capacity + arrival
    placing = (
        jnp.arange(blocks * capacity, dtype=jnp.int32)[:, None] == slot_index[None, :]
    ).astype(jnp.bfloat16)
    placed = jnp.dot(placing, white_traces, preferred_element_type=jnp.float32)
    placed = placed.reshape(blocks, capacity, 2, folds, PERIOD)
    bin_index = jnp.arange(PERIOD, dtype=jnp.int32)
    lag_value = (jnp.arange(lags_out, dtype=jnp.int32) - lags_out // 2) * DEC
    phase_angle = jnp.mod(bin_index[:, None] * lag_value[None, :], BINS).astype(jnp.float32) * (
        2.0 * math.pi / BINS
    )
    table = jnp.concatenate([jnp.cos(phase_angle), jnp.sin(phase_angle)], axis=0).astype(
        jnp.bfloat16
    )
    norm_scale = BINS ** (-0.5)
    real_s = white_sources[:, None, :, 0]
    imag_s = white_sources[:, None, :, 1]
    cross = []
    for offset in range(offsets):
        visiting = jnp.roll(placed, offset, axis=0)
        real_t = visiting[:, :, None, 0]
        imag_t = visiting[:, :, None, 1]
        even = jnp.sum(real_t * real_s + imag_t * imag_s, axis=3)
        odd = jnp.sum(real_t * imag_s - imag_t * real_s, axis=3)
        cross.append(jnp.concatenate([even, odd], axis=-1))
    cross = jnp.stack(cross, axis=1).astype(jnp.bfloat16)
    rows = blocks * offsets * capacity * source_count
    partial = jnp.dot(cross.reshape(rows, 2 * PERIOD), table, preferred_element_type=jnp.float32)
    partial = (partial * norm_scale).astype(jnp.bfloat16)
    partial = partial.reshape(blocks, offsets, capacity, source_count, lags_out)
    arrived = lax.all_to_all(partial, "blk", split_axis=0, concat_axis=0, tiled=True)
    summed = lax.psum_scatter(arrived.astype(jnp.float32), "band", scatter_dimension=0, tiled=True)
    half = summed.shape[0]
    return jnp.transpose(summed, (3, 1, 0, 2, 4)).reshape(
        source_count, offsets, half * capacity, lags_out
    )


def solution(mesh):
    placed = (P("blk", None, "band"), P("blk", None, "band"), P("blk", None))
    return jax.shard_map(
        per_device,
        mesh=mesh,
        in_specs=placed,
        out_specs=P("blk", None, "band", None),
        check_vma=False,
    )
```

profile of v0, /device:TPU:0, one launch (start us, length us, event | category | flops | bytes accessed | tf_op | source)
XLA Modules:
  0.0 150.7 jit_solution(14130566093052021480)
XLA Ops:
  6.5 0.0 reduce-scatter.2.cloned.1.call-start
  6.5 45.7 %all_gather.3 = bf16[32,2,4096]{2,1,0:T(2,128)(2,1)S(1)} all-gather(bf16[2,2,4096]{2,1,0:T(2,128)(2,1)} %param.4), channel_id=1, replica_groups=mesh['blk'=16,'band'=2] {'blk'}, dimensions={0}, use_global_device_ids=true | all-gather | bytes 557056 | tf_op jit(solution)/shard_map/all_gather | solution.py:23
  52.2 0.8 copy-done.4
  53.0 0.8 fusion.12
  53.8 2.8 %fusion = f32[64]{0:T(128)S(1)} fusion(bf16[64,2,4096]{2,1,0:T(2,128)(2,1)} %param.3), kind=kLoop, calls=%fused_computation.17 | loop fusion | flops 1572800 | bytes 1048832 | tf_op jit(solution)/shard_map/reduce_sum | solution.py:28
  56.6 2.5 %all-reduce = (f32[32]{0:T(128)S(1)}, f32[64]{0:T(128)S(1)}) all-reduce(f32[32]{0:T(128)S(1)} %fusion.12, f32[64]{0:T(128)S(1)} %fusion), channel_id=1, replica_groups=mesh['blk'=16,'band'=2] {'band'}, use_global_device_ids=true, to_apply=%region_5.6 | all-reduce | flops 96 | bytes 768 | tf_op jit(solution)/shard_map/psum | solution.py:26
  59.1 2.5 %fusion.1 = bf16[64,2,4096]{2,1,0:T(2,128)(2,1)S(1)} fusion(bf16[64,2,4096]{2,1,0:T(2,128)(2,1)} %param.3, f32[64]{0:T(128)S(1)} %add_rsqrt_fusion.1), kind=kLoop, calls=%fused_computation.18 | loop fusion | flops 1572864 | bytes 2097408 | tf_op jit(solution)/shard_map/convert_element_type | solution.py:35
  61.6 0.6 copy.44
  62.2 0.0 copy-done.8
  62.2 0.1 fusion.26
  62.3 0.1 reduce_window_sum.11
  62.4 0.2 select_reduce_fusion
  62.6 0.7 fusion.24
  63.3 0.2 slice.107
  63.5 0.9 slice.106
  64.5 2.1 %slice.103 = f32[112,8192]{1,0:T(8,128)} slice(f32[128,8192]{1,0:T(8,128)S(1)} %fusion.24), slice={[0:112], [0:8192]} | slice | bytes 7340032 | tf_op jit(solution)/shard_map/jit(_roll_static)/slice | solution.py:67
  66.6 0.8 slice.102
  67.4 2.1 %slice.99 = f32[120,8192]{1,0:T(8,128)} slice(f32[128,8192]{1,0:T(8,128)S(1)} %fusion.24), slice={[0:120], [0:8192]} | slice | bytes 7864320 | tf_op jit(solution)/shard_map/jit(_roll_static)/slice | solution.py:67
  69.6 0.7 slice.98
  70.3 2.4 %slice_bitcast_fusion.1 = (f32[16,8,4,1024]{3,1,2,0:T(8,128)}, f32[16,8,4,1024]{3,1,2,0:T(8,128)}) fusion(f32[16,8,2,4,1024]{4,1,3,2,0:T(8,128)S(1)} %bitcast.46), kind=kLoop, calls=%fused_computation.32 | loop fusion | bytes 8388608 | tf_op jit(solution)/shard_map/mul | solution.py:70
  72.7 0.0 copy-done.5
  72.7 1.5 %fusion.23 = f32[32,2,4096]{2,1,0:T(2,128)} fusion(f32[32]{0:T(128)S(1)} %add_rsqrt_fusion, bf16[32,2,4096]{2,1,0:T(2,128)(2,1)S(1)} %copy-done.5), kind=kLoop, calls=%fused_computation.57 | loop fusion | flops 1048576 | bytes 1572992 | tf_op jit(solution)/shard_map/reshape | solution.py:42
  74.2 3.3 %reshape.51 = f32[16,2,2,4,1024]{4,3,2,1,0:T(4,128)} reshape(f32[32,2,4096]{2,1,0:T(2,128)} %fusion.23) | data formatting | bytes 2097152 | tf_op jit(solution)/shard_map/reshape | solution.py:42
  77.6 1.3 slice_bitcast_fusion.3
  78.9 1.6 %fusion.3 = (f32[16,8,4,1024]{3,1,2,0:T(8,128)S(1)}, f32[16,8,4,1024]{3,1,2,0:T(8,128)S(1)}) fusion(f32[3,8,2,4,1024]{4,1,3,2,0:T(8,128)} %bitcast.52, f32[13,8,2,4,1024]{4,1,3,2,0:T(8,128)S(1)} %bitcast.49), kind=kLoop, calls=%fused_computation.20 | loop fusion | flops 1048576 | bytes 8388608 | tf_op jit(solution)/shard_map/mul | solution.py:70
  80.5 0.6 copy-done.1
  81.2 0.1 copy-done.6
  81.3 0.5 fusion.5
  81.8 1.6 %copy-done = f32[120,8192]{1,0:T(8,128)S(1)} copy-done((f32[120,8192]{1,0:T(8,128)S(1)}, f32[120,8192]{1,0:T(8,128)}, u32[]{:S(2)}) %copy-start) | copy-done | bytes 3932184
  83.4 0.0 copy-done.7
  83.4 0.5 fusion.7
  83.9 1.1 copy-done.2
  85.0 0.6 copy-done.3
  85.6 7.3 %add_reduce_fusion.3 = (bf16[16,8,2,1024]{3,1,2,0:T(8,128)(2,1)S(1)}, bf16[16,8,2,1024]{3,1,2,0:T(8,128)(2,1)S(1)}, bf16[16,8,2,1024]{3,1,2,0:T(8,128)(2,1)S(1)}...) fusion(f32[16,2,4,1024]{3,2,1,0:T(4,128)S(1)} %get-tuple-elemen, ...), kind=kLoop, calls=%fused_computation.14 | loop fusion | flops 31457280 | bytes 22020096 | tf_op jit(solution)/shard_map/reduce_sum | solution.py:70
  92.9 0.2 maximum_bitcast_fusion
  93.1 0.2 maximum_bitcast_fusion.2
  93.3 0.6 pad_maximum_fusion
  93.9 6.3 %copy.41 = bf16[16,4,8,2,2048]{4,3,2,1,0:T(2,128)(2,1)} copy(bf16[16,4,8,2,2048]{4,2,3,0,1:T(8,128)(2,1)S(1)} %pad_maximum_fusion) | data formatting | bytes 8388608 | tf_op jit(solution)/shard_map/stack | solution.py:73
  100.2 7.2 %convert_element_type.39 = bf16[1024,2048]{1,0:T(8,128)(2,1)} reshape(bf16[16,4,8,2,2048]{4,3,2,1,0:T(2,128)(2,1)} %copy.41) | data formatting | bytes 8388608 | tf_op jit(solution)/shard_map/convert_element_type | solution.py:73
  107.4 4.4 %cosine_convert_fusion = (bf16[1024,256]{1,0:T(8,128)(2,1)S(1)}, bf16[1024,256]{1,0:T(8,128)(2,1)S(1)}) fusion(s32[256]{0:T(256)S(1)} %add_multiply_fusion), kind=kLoop, calls=%fused_computation.53 | loop fusion | flops 4194304 | bytes 1049600 | tf_op jit(solution)/shard_map/convert.1
  111.8 3.4 %fusion.11 = bf16[1024,256]{1,0:T(8,128)(2,1)S(1)} fusion(bf16[1024,2048]{1,0:T(8,128)(2,1)} %convert_element_type.39, bf16[1024,256]{1,0:T(8,128)(2,1)S(1)} %get-tuple-element.32, bf16[1024,256]{1,0:T(8,128)(2,1)S(1)} %get-tuple-element.31), kind=kOutput, calls=%fused_computation.39 | convolution fusion | flops 1076363264 | bytes 5767168 | tf_op jit(solution)/shard_map/dot_general | solution.py:75
  115.2 0.2 reshape.48
  115.4 0.1 copy.42
  115.5 18.1 %all_to_all.5 = bf16[16,4,8,2,256]{4,2,3,1,0:T(8,128)(2,1)S(1)} all-to-all(bf16[16,4,8,2,256]{4,2,3,1,0:T(8,128)(2,1)S(1)} %copy.42), channel_id=1, replica_groups=mesh['blk'=16,'band'=2] {'blk'}, dimensions={0} | all-to-all | bytes 1048576 | tf_op jit(solution)/shard_map/all_to_all | solution.py:78
  133.6 1.1 convert_element_type.42
  134.7 0.0 reduce-scatter.2.cloned.1.call-update
  134.8 7.2 %reduce-scatter.2.cloned.1.call-done = f32[8,4,8,2,256]{4,2,3,1,0:T(8,128)} async-done(((f32[16,4,8,2,256]{4,2,3,1,0:T(8,128)}), f32[8,4,8,2,256]{4,2,3,1,0:T(8,128)}) %reduce-scatter.2.cloned.1.call-update) | async-done | bytes 524304 | tf_op jit(solution)/shard_map/reduce_scatter | solution.py:79
  142.0 1.9 %copy.46 = f32[8,4,8,2,256]{4,2,0,1,3:T(8,128)} copy(f32[8,4,8,2,256]{4,2,3,1,0:T(8,128)} %reduce-scatter.2.cloned.1.call-done) | data formatting | bytes 1048576 | tf_op jit(solution)/shard_map/reduce_scatter | solution.py:79
  (13 shorter events, 0.0 us)
Async XLA Ops:
  6.5 55.7 %copy-start.8 = (s32[64,1]{0,1:T(1,128)S(1)}, s32[64,1]{0,1:T(1,128)}, u32[]{:S(2)}) copy-start(s32[64,1]{0,1:T(1,128)} %param.5) | copy-start | bytes 772
  6.5 135.4 %reduce-scatter.2.cloned.1.call-start = ((), (), s32[]{:S(2)}) async-start(), calls=%async_computation.2 | async-start | bytes 1572864 | tf_op jit(solution)/shard_map/reduce_scatter | solution.py:79
  52.2 0.8 copy-start.4
  70.3 2.4 %copy-start.5 = (bf16[32,2,4096]{2,1,0:T(2,128)(2,1)S(1)}, bf16[32,2,4096]{2,1,0:T(2,128)(2,1)}, u32[]{:S(2)}) copy-start(bf16[32,2,4096]{2,1,0:T(2,128)(2,1)} %copy-done.4) | copy-start | bytes 1572868
  78.9 2.3 %copy-start.1 = (f32[112,8192]{1,0:T(8,128)S(1)}, f32[112,8192]{1,0:T(8,128)}, u32[]{:S(2)}) copy-start(f32[112,8192]{1,0:T(8,128)} %slice.103) | copy-start | bytes 11010052
  78.9 2.4 %copy-start.6 = (f32[16,8192]{1,0:T(8,128)S(1)}, f32[16,8192]{1,0:T(8,128)}, u32[]{:S(2)}) copy-start(f32[16,8192]{1,0:T(8,128)} %slice.102) | copy-start | bytes 1572868
  81.3 2.1 %copy-start = (f32[120,8192]{1,0:T(8,128)S(1)}, f32[120,8192]{1,0:T(8,128)}, u32[]{:S(2)}) copy-start(f32[120,8192]{1,0:T(8,128)} %slice.99) | copy-start | bytes 11796484
  81.3 2.1 %copy-start.7 = (f32[8,8192]{1,0:T(8,128)S(1)}, f32[8,8192]{1,0:T(8,128)}, u32[]{:S(2)}) copy-start(f32[8,8192]{1,0:T(8,128)} %slice.98) | copy-start | bytes 786436
  83.4 1.6 %copy-start.2 = (f32[16,8,4,1024]{3,1,2,0:T(8,128)S(1)}, f32[16,8,4,1024]{3,1,2,0:T(8,128)}, u32[]{:S(2)}) copy-start(f32[16,8,4,1024]{3,1,2,0:T(8,128)} %get-tuple-element.27) | copy-start | bytes 6291460
  83.4 2.2 %copy-start.3 = (f32[16,8,4,1024]{3,1,2,0:T(8,128)S(1)}, f32[16,8,4,1024]{3,1,2,0:T(8,128)}, u32[]{:S(2)}) copy-start(f32[16,8,4,1024]{3,1,2,0:T(8,128)} %get-tuple-element.28) | copy-start | bytes 6291460
Sparse Core Ops, SparseCore 0:
  134.9 7.0 reduce-scatter.1
where the time goes:
time: 151 us
  blocking collectives  66.2 us (44%)
  local copies, waits for them, and re-layouts  35.1 us (23%)
  other arithmetic  24.5 us (16%)
  between operations  13.6 us (9%)
  waiting for transfers between devices  7.22 us (5%)
  matrix products  4.13 us (3%)
    all_gather x1, blocking collectives, per_device(): all_sources = lax.all_gather(sources, 'blk', axis=0, tiled=True)  45.7 us
    all_to_all x1, blocking collectives, per_device(): lax.all_to_all(partial, 'blk', split_axis=0, concat_axis=0, tiled=True)  18.1 us
    reduce_sum x1, other arithmetic, per_device(): even = jnp.sum(real_t * real_s + imag_t * imag_s, axis=3)  7.3 us
    reduce_scatter x1, waiting for transfers between devices, per_device(): lax.psum_scatter(arrived.astype(jnp.float32), 'band', scatter_dimension=0...  7.2 us
    convert_element_type x1, local copies, waits for them, and re-layouts, per_device(): cross = jnp.stack(cross, axis=1).astype(jnp.bfloat16)  7.2 us
    slice x6, local copies, waits for them, and re-layouts, per_device(): visiting = jnp.roll(placed, offset, axis=0)  6.99 us
    another operation x1, local copies, waits for them, and re-layouts, per_device(): cross = jnp.stack(cross, axis=1).astype(jnp.bfloat16)  6.3 us
    unnamed x19, local copies, waits for them, and re-layouts  5.42 us
  transfers between devices with their start and end apart: 1, of which 1 were waited for; matrix products, arithmetic and copies ran while one was open for 0% of the time, Pallas kernels for 0%

commit v1 on v0

--- a/solution.py
+++ b/solution.py
@@ -11,6 +11,18 @@
 EPS = 1e-06
 
 
+def doubled_up(array, axis, dim):
+    ways, here, step = (lax.axis_size(axis), lax.axis_index(axis), array.shape[dim])
+    line, have = (array, 1)
+    while have < ways:
+        line = jnp.concatenate(
+            [line, lax.ppermute(line, axis, [(d, (d - have) % ways) for d in range(ways)])],
+            axis=dim,
+        )
+        have = 2 * have
+    return jnp.roll(line, here * step, axis=dim)
+
+
 def per_device(traces, sources, owner):
     blocks = lax.axis_size("blk")
     station_count = traces.shape[0]
@@ -20,7 +32,7 @@
     capacity = max(2, 2 * station_count // blocks)
     lags_out = LAGS // DEC
     offsets = blocks // 4
-    all_sources = lax.all_gather(sources, "blk", axis=0, tiled=True)
+    all_sources = doubled_up(sources, "blk", 0)
     trace_float = traces.astype(jnp.float32)
     all_source_float = all_sources.astype(jnp.float32)
     trace_power, source_power = lax.psum(

time: 151 us -> 140 us (0.927)
  blocking collectives: 66.2 us -> 22.7 us
  waiting for transfers between devices: 7.22 us -> 26.7 us
  starting transfers between devices: 0.01 us -> 8.07 us
  other arithmetic: 24.5 us -> 27.1 us
  local copies, waits for them, and re-layouts: 35.1 us -> 37.2 us
    all_gather x1 -> x0, blocking collectives: 45.7 us -> none  [per_device(): all_sources = lax.all_gather(sources, 'blk', axis=0, tiled=True)]
    ppermute x0 -> x4, waiting for transfers between devices: none -> 19.7 us  [doubled_up(): lax.ppermute(line, axis, [(d, (d - have) % ways) for d in range(ways)])]
    ppermute x0 -> x4, starting transfers between devices: none -> 8.06 us  [doubled_up(): lax.ppermute(line, axis, [(d, (d - have) % ways) for d in range(ways)])]
    concatenate x0 -> x3, other arithmetic: none -> 2.91 us  [doubled_up(): jnp.concatenate([line, lax.ppermute(line, axis, [(d, (d - have) % ways) f...]
    all_to_all x1, blocking collectives: 18.1 us -> 20.1 us  [per_device(): lax.all_to_all(partial, 'blk', split_axis=0, concat_axis=0, tiled=True)]
    mul x3, other arithmetic: 2.66 us -> 0.92 us  [per_device(): even = jnp.sum(real_t * real_s + imag_t * imag_s, axis=3)]
    unnamed x19 -> x34, local copies, waits for them, and re-layouts: 5.42 us -> 6.19 us
  transfers between devices with their start and end apart: 1 -> 5, of which waited for: 1 -> 4; matrix products, arithmetic and copies ran while one was open for 0% -> 8% of each run, Pallas kernels for 0% -> 0%
where the time goes in v1:
time: 140 us; the launch traced here: 139 us
  local copies, waits for them, and re-layouts  37.2 us (27%)
  other arithmetic  27.1 us (19%)
  waiting for transfers between devices  26.7 us (19%)
  blocking collectives  22.7 us (16%)
  between operations  13.6 us (10%)
  starting transfers between devices  8.07 us (6%)
  matrix products  4.12 us (3%)
    all_to_all x1, blocking collectives, per_device(): lax.all_to_all(partial, 'blk', split_axis=0, concat_axis=0, tiled=True)  20.1 us
    ppermute x4, waiting for transfers between devices, doubled_up(): lax.ppermute(line, axis, [(d, (d - have) % ways) for d in range(ways)])  19.7 us
    ppermute x4, starting transfers between devices, doubled_up(): lax.ppermute(line, axis, [(d, (d - have) % ways) for d in range(ways)])  8.06 us
    slice x6, local copies, waits for them, and re-layouts, per_device(): visiting = jnp.roll(placed, offset, axis=0)  7.36 us
    reduce_sum x1, other arithmetic, per_device(): even = jnp.sum(real_t * real_s + imag_t * imag_s, axis=3)  7.35 us
    convert_element_type x1, local copies, waits for them, and re-layouts, per_device(): cross = jnp.stack(cross, axis=1).astype(jnp.bfloat16)  7.3 us
    reduce_scatter x1, waiting for transfers between devices, per_device(): lax.psum_scatter(arrived.astype(jnp.float32), 'band', scatter_dimension=0...  7.01 us
    another operation x1, local copies, waits for them, and re-layouts, per_device(): cross = jnp.stack(cross, axis=1).astype(jnp.bfloat16)  6.34 us
  transfers between devices with their start and end apart: 5, of which 4 were waited for; matrix products, arithmetic and copies ran while one was open for 8% of the time, Pallas kernels for 0%

profile of v1, /device:TPU:0, one launch (start us, length us, event | category | flops | bytes accessed | tf_op | source)
XLA Modules:
  0.0 139.4 jit_solution(5224378693188938661)
XLA Ops:
  6.5 6.9 %collective-permute-start = (bf16[2,2,4096]{2,1,0:T(2,128)(2,1)}, bf16[2,2,4096]{2,1,0:T(2,128)(2,1)S(1)}, u32[]{:S(2)}, u32[]{:S(2)}) collective-permute-start(bf16[2,2,4096]{2,1,0:T(2,128)(2,1)} %param.4), channel_id=1, source_target_pairs={{0,30},{2,0},{4,2},{6,4},{8,6},{10,8},{12,10},{14,12},{16,14},{18,... | collective-permute-start | bytes 98312 | tf_op jit(solution)/shard_map/ppermute | solution.py:19
  13.5 0.8 constant_dynamic-update-slice_fusion.9
  14.3 2.8 %fusion = f32[64]{0:T(128)S(1)} fusion(bf16[64,2,4096]{2,1,0:T(2,128)(2,1)} %param.3), kind=kLoop, calls=%fused_computation.17 | loop fusion | flops 1572800 | bytes 1048832 | tf_op jit(solution)/shard_map/reduce_sum | solution.py:40
  17.1 0.7 fusion.26
  17.9 0.8 select_reduce_fusion
  18.8 5.0 %cosine_convert_fusion = (bf16[1024,256]{1,0:T(8,128)(2,1)}, bf16[1024,256]{1,0:T(8,128)(2,1)}) fusion(s32[256]{0:T(256)S(1)} %add_multiply_fusion), kind=kLoop, calls=%fused_computation.53 | loop fusion | flops 4194304 | bytes 1049600 | tf_op jit(solution)/shard_map/convert.1
  23.8 0.7 multiply_add_fusion
  24.5 0.8 pad_maximum_fusion.6
  25.3 0.6 collective-permute-start.1
  25.9 3.7 %collective-permute-done.1 = bf16[4,2,4096]{2,1,0:T(2,128)(2,1)S(1)} collective-permute-done((bf16[4,2,4096]{2,1,0:T(2,128)(2,1)S(1)}, bf16[4,2,4096]{2,1,0:T(2,128)(2,1)S(1)}, u32[]{:S(2)}, u32[]{:S(2)}) %collective-permute-start.1) | collective-permute-done | bytes 65568 | tf_op jit(solution)/shard_map/ppermute | solution.py:19
  29.6 0.9 pad_maximum_fusion.5
  30.6 0.5 collective-permute-start.2
  31.1 4.5 %collective-permute-done.2 = bf16[8,2,4096]{2,1,0:T(2,128)(2,1)S(1)} collective-permute-done((bf16[8,2,4096]{2,1,0:T(2,128)(2,1)S(1)}, bf16[8,2,4096]{2,1,0:T(2,128)(2,1)S(1)}, u32[]{:S(2)}, u32[]{:S(2)}) %collective-permute-start.2) | collective-permute-done | bytes 131104 | tf_op jit(solution)/shard_map/ppermute | solution.py:19
  35.6 1.1 pad_maximum_fusion.4
  36.9 11.5 %collective-permute-done.3 = bf16[16,2,4096]{2,1,0:T(2,128)(2,1)S(1)} collective-permute-done((bf16[16,2,4096]{2,1,0:T(2,128)(2,1)S(1)}, bf16[16,2,4096]{2,1,0:T(2,128)(2,1)S(1)}, u32[]{:S(2)}, u32[]{:S(2)}) %collective-permute-start.3) | collective-permute-done | bytes 262176 | tf_op jit(solution)/shard_map/ppermute | solution.py:19
  48.4 0.2 constant_dynamic-update-slice_fusion.5
  48.9 0.2 constant_dynamic-update-slice_fusion
  49.1 0.8 fusion.12
  49.9 2.6 %all-reduce = (f32[32]{0:T(128)S(1)}, f32[64]{0:T(128)S(1)}) all-reduce(f32[32]{0:T(128)S(1)} %fusion.12, f32[64]{0:T(128)S(1)} %fusion), channel_id=1, replica_groups=mesh['blk'=16,'band'=2] {'band'}, use_global_device_ids=true, to_apply=%region_5.6 | all-reduce | flops 96 | bytes 768 | tf_op jit(solution)/shard_map/psum | solution.py:38
  52.6 1.3 fusion.1
  53.9 0.6 copy.44
  54.5 0.7 fusion.24
  55.2 0.8 slice.98
  56.0 2.4 %slice.99 = f32[120,8192]{1,0:T(8,128)} slice(f32[128,8192]{1,0:T(8,128)S(1)} %fusion.24), slice={[0:120], [0:8192]} | slice | bytes 7864320 | tf_op jit(solution)/shard_map/jit(_roll_static)/slice | solution.py:79
  58.4 0.8 slice.102
  59.2 2.2 %slice.103 = f32[112,8192]{1,0:T(8,128)} slice(f32[128,8192]{1,0:T(8,128)S(1)} %fusion.24), slice={[0:112], [0:8192]} | slice | bytes 7340032 | tf_op jit(solution)/shard_map/jit(_roll_static)/slice | solution.py:79
  61.4 0.9 slice.106
  62.3 0.2 slice.107
  62.6 1.0 copy-done.7
  63.6 1.5 %fusion.23 = f32[32,2,4096]{2,1,0:T(2,128)} fusion(f32[32]{0:T(128)S(1)} %add_rsqrt_fusion, bf16[64,2,4096]{2,1,0:T(2,128)(2,1)S(1)} %copy-done.7, s32[]{:T(128)S(6)} %select_n.22), kind=kLoop, calls=%fused_computation.57 | loop fusion | flops 1048576 | bytes 1572996 | tf_op jit(solution)/shard_map/reshape | solution.py:54
  65.1 3.3 %reshape.51 = f32[16,2,2,4,1024]{4,3,2,1,0:T(4,128)} reshape(f32[32,2,4096]{2,1,0:T(2,128)} %fusion.23) | data formatting | bytes 2097152 | tf_op jit(solution)/shard_map/reshape | solution.py:54
  68.4 1.3 slice_bitcast_fusion.3
  69.8 2.9 %slice_bitcast_fusion.1 = (f32[16,8,4,1024]{3,1,2,0:T(8,128)S(1)}, f32[16,8,4,1024]{3,1,2,0:T(8,128)S(1)}) fusion(f32[16,8,2,4,1024]{4,1,3,2,0:T(8,128)} %bitcast.46), kind=kLoop, calls=%fused_computation.32 | loop fusion | bytes 8388608 | tf_op jit(solution)/shard_map/mul | solution.py:82
  72.7 0.4 copy-done.1
  73.2 0.3 fusion.7
  73.5 1.7 %copy-done.2 = f32[112,8192]{1,0:T(8,128)S(1)} copy-done((f32[112,8192]{1,0:T(8,128)S(1)}, f32[112,8192]{1,0:T(8,128)}, u32[]{:S(2)}) %copy-start.2) | copy-done | bytes 3670040
  75.3 0.3 fusion.5
  75.6 0.8 copy-done.4
  76.4 0.3 fusion.3
  76.7 7.3 %add_reduce_fusion.3 = (bf16[16,8,2,1024]{3,1,2,0:T(8,128)(2,1)S(1)}, bf16[16,8,2,1024]{3,1,2,0:T(8,128)(2,1)S(1)}, bf16[16,8,2,1024]{3,1,2,0:T(8,128)(2,1)S(1)}...) fusion(f32[16,2,4,1024]{3,2,1,0:T(4,128)S(1)} %get-tuple-elemen, ...), kind=kLoop, calls=%fused_computation.14 | loop fusion | flops 31457280 | bytes 22020096 | tf_op jit(solution)/shard_map/reduce_sum | solution.py:82
  84.5 0.6 pad_maximum_fusion
  85.1 6.3 %copy.41 = bf16[16,4,8,2,2048]{4,3,2,1,0:T(2,128)(2,1)} copy(bf16[16,4,8,2,2048]{4,2,3,0,1:T(8,128)(2,1)S(1)} %pad_maximum_fusion) | data formatting | bytes 8388608 | tf_op jit(solution)/shard_map/stack | solution.py:85
  91.4 7.3 %convert_element_type.39 = bf16[1024,2048]{1,0:T(8,128)(2,1)} reshape(bf16[16,4,8,2,2048]{4,3,2,1,0:T(2,128)(2,1)} %copy.41) | data formatting | bytes 8388608 | tf_op jit(solution)/shard_map/convert_element_type | solution.py:85
  98.7 3.4 %fusion.11 = bf16[1024,256]{1,0:T(8,128)(2,1)S(1)} fusion(bf16[1024,2048]{1,0:T(8,128)(2,1)} %convert_element_type.39, bf16[1024,256]{1,0:T(8,128)(2,1)S(1)} %copy-done.11, bf16[1024,256]{1,0:T(8,128)(2,1)S(1)} %copy-done.10), kind=kOutput, calls=%fused_computation.39 | convolution fusion | flops 1076363264 | bytes 5767168 | tf_op jit(solution)/shard_map/dot_general | solution.py:87
  102.5 20.1 %all_to_all.5 = bf16[16,4,8,2,256]{4,2,3,1,0:T(8,128)(2,1)S(1)} all-to-all(bf16[16,4,8,2,256]{4,2,3,1,0:T(8,128)(2,1)S(1)} %copy.42), channel_id=1, replica_groups=mesh['blk'=16,'band'=2] {'blk'}, dimensions={0} | all-to-all | bytes 1048576 | tf_op jit(solution)/shard_map/all_to_all | solution.py:90
  122.6 1.1 convert_element_type.42
  123.7 7.0 %reduce-scatter.2.cloned.1.call-done = f32[8,4,8,2,256]{4,2,3,1,0:T(8,128)} async-done(((f32[16,4,8,2,256]{4,2,3,1,0:T(8,128)}), f32[8,4,8,2,256]{4,2,3,1,0:T(8,128)}) %reduce-scatter.2.cloned.1.call-update) | async-done | bytes 524304 | tf_op jit(solution)/shard_map/reduce_scatter | solution.py:91
  130.7 1.9 %copy.46 = f32[8,4,8,2,256]{4,2,0,1,3:T(8,128)} copy(f32[8,4,8,2,256]{4,2,3,1,0:T(8,128)} %reduce-scatter.2.cloned.1.call-done) | data formatting | bytes 1048576 | tf_op jit(solution)/shard_map/reduce_scatter | solution.py:91
  (39 shorter events, 1.5 us)
Async XLA Ops:
  6.5 42.1 %copy-start.9 = (bf16[2,2,4096]{2,1,0:T(2,128)(2,1)S(1)}, bf16[2,2,4096]{2,1,0:T(2,128)(2,1)}, u32[]{:S(2)}) copy-start(bf16[2,2,4096]{2,1,0:T(2,128)(2,1)} %param.4) | copy-start | bytes 98308
  6.5 46.0 %copy-start.3 = (bf16[64,2,4096]{2,1,0:T(2,128)(2,1)S(1)}, bf16[64,2,4096]{2,1,0:T(2,128)(2,1)}, u32[]{:S(2)}) copy-start(bf16[64,2,4096]{2,1,0:T(2,128)(2,1)} %param.3) | copy-start | bytes 3145732
  6.5 124.2 %reduce-scatter.2.cloned.1.call-start = ((), (), s32[]{:S(2)}) async-start(), calls=%async_computation.2 | async-start | bytes 1572864 | tf_op jit(solution)/shard_map/reduce_scatter | solution.py:91
  6.5 17.9 %collective-permute-start = (bf16[2,2,4096]{2,1,0:T(2,128)(2,1)}, bf16[2,2,4096]{2,1,0:T(2,128)(2,1)S(1)}, u32[]{:S(2)}, u32[]{:S(2)}) collective-permute-start(bf16[2,2,4096]{2,1,0:T(2,128)(2,1)} %param.4), channel_id=1, source_target_pairs={{0,30},{2,0},{4,2},{6,4},{8,6},{10,8},{12,10},{14,12},{16,14},{18,... | collective-permute-start | bytes 98312 | tf_op jit(solution)/shard_map/ppermute | solution.py:19
  25.3 4.3 %collective-permute-start.1 = (bf16[4,2,4096]{2,1,0:T(2,128)(2,1)S(1)}, bf16[4,2,4096]{2,1,0:T(2,128)(2,1)S(1)}, u32[]{:S(2)}, u32[]{:S(2)}) collective-permute-start(bf16[4,2,4096]{2,1,0:T(2,128)(2,1)S(1)} %pad_maximum_fusion.6), channel_id=1, source_target_pairs={{0,28},{2,30},{4,0},{6,2},{8,4},{10,6},{12,8},{14,10},{16,12},{18,... | collective-permute-start | bytes 196616 | tf_op jit(solution)/shard_map/ppermute | solution.py:19
  30.6 5.0 %collective-permute-start.2 = (bf16[8,2,4096]{2,1,0:T(2,128)(2,1)S(1)}, bf16[8,2,4096]{2,1,0:T(2,128)(2,1)S(1)}, u32[]{:S(2)}, u32[]{:S(2)}) collective-permute-start(bf16[8,2,4096]{2,1,0:T(2,128)(2,1)S(1)} %pad_maximum_fusion.5), channel_id=1, source_target_pairs={{0,24},{2,26},{4,28},{6,30},{8,0},{10,2},{12,4},{14,6},{16,8},{18,... | collective-permute-start | bytes 393224 | tf_op jit(solution)/shard_map/ppermute | solution.py:19
  36.7 11.7 %collective-permute-start.3 = (bf16[16,2,4096]{2,1,0:T(2,128)(2,1)S(1)}, bf16[16,2,4096]{2,1,0:T(2,128)(2,1)S(1)}, u32[]{:S(2)}, u32[]{:S(2)}) collective-permute-start(bf16[16,2,4096]{2,1,0:T(2,128)(2,1)S(1)} %pad_maximum_fusion.4), channel_id=1, source_target_pairs={{0,16},{2,18},{4,20},{6,22},{8,24},{10,26},{12,28},{14,30},{16,0},... | collective-permute-start | bytes 786440 | tf_op jit(solution)/shard_map/ppermute | solution.py:19
  49.1 6.1 %copy-start.6 = (bf16[64,2,4096]{2,1,0:T(2,128)(2,1)}, bf16[64,2,4096]{2,1,0:T(2,128)(2,1)S(1)}, u32[]{:S(2)}) copy-start(bf16[64,2,4096]{2,1,0:T(2,128)(2,1)S(1)} %constant_dynamic-update-slice_fusion) | copy-start | bytes 3145732
  55.2 7.1 %copy-start = (f32[128,8192]{1,0:T(8,128)}, f32[128,8192]{1,0:T(8,128)S(1)}, u32[]{:S(2)}) copy-start(f32[128,8192]{1,0:T(8,128)S(1)} %fusion.24) | copy-start | bytes 12582916
  62.3 1.2 copy-start.7
  69.8 3.4 %copy-start.1 = (f32[120,8192]{1,0:T(8,128)S(1)}, f32[120,8192]{1,0:T(8,128)}, u32[]{:S(2)}) copy-start(f32[120,8192]{1,0:T(8,128)} %slice.99) | copy-start | bytes 11796484
  69.8 3.4 %copy-start.8 = (f32[8,8192]{1,0:T(8,128)S(1)}, f32[8,8192]{1,0:T(8,128)}, u32[]{:S(2)}) copy-start(f32[8,8192]{1,0:T(8,128)} %slice.98) | copy-start | bytes 786436
  73.2 2.0 %copy-start.2 = (f32[112,8192]{1,0:T(8,128)S(1)}, f32[112,8192]{1,0:T(8,128)}, u32[]{:S(2)}) copy-start(f32[112,8192]{1,0:T(8,128)} %slice.103) | copy-start | bytes 11010052
  73.2 2.1 %copy-start.5 = (f32[16,8192]{1,0:T(8,128)S(1)}, f32[16,8192]{1,0:T(8,128)}, u32[]{:S(2)}) copy-start(f32[16,8192]{1,0:T(8,128)} %slice.102) | copy-start | bytes 1572868
  75.3 1.1 copy-start.4
  91.4 7.3 %copy-start.10 = (bf16[1024,256]{1,0:T(8,128)(2,1)S(1)}, bf16[1024,256]{1,0:T(8,128)(2,1)}, u32[]{:S(2)}) copy-start(bf16[1024,256]{1,0:T(8,128)(2,1)} %get-tuple-element.31) | copy-start | bytes 1572868
  91.4 7.3 %copy-start.11 = (bf16[1024,256]{1,0:T(8,128)(2,1)S(1)}, bf16[1024,256]{1,0:T(8,128)(2,1)}, u32[]{:S(2)}) copy-start(bf16[1024,256]{1,0:T(8,128)(2,1)} %get-tuple-element.32) | copy-start | bytes 1572868
Sparse Core Ops, SparseCore 0:
  123.8 6.8 reduce-scatter.1
